TPU v7x, 128 devices: a whole 4x4x4 slice. The times are simulated.
128 devices in a mesh: seq: 32 (over x, y_hi, z), mp: 4 (over y_lo, core).
Axes of the slice: x: 4, y: 4 (y_hi: 2, y_lo: 2; y = y_hi * 2 + y_lo), z: 4, core: 2. Of those that a mesh axis runs over, the one named last changes fastest.
Arguments:
- hidden_in: bfloat16 [8192, 1536], P('seq', 'mp'), may hold values from -6 to 6
- wq: bfloat16 [1536, 1536], P('seq', 'mp'), may hold values from -1 to 1
- wkv: bfloat16 [1536, 512], P('seq'), may hold values from -0.15625 to 0.15625
- wo: bfloat16 [1536, 1536], P('mp', 'seq'), may hold values from -0.15625 to 0.15625
- lengths: int32 [3], replicated, may hold values from 1 to 6144, 8192 in all
- routes: int32 [8192, 4], P('seq'), may hold values from 0 to 31, all different within a row; in each aligned block of 256 rows (0 to 255, 256 to 511, ...) at most 64 rows name the same one
- gate_logits: float32 [8192, 4], P('seq'), may hold values from -6 to 6
- expert_gate: bfloat16 [32, 768, 1536], P('seq', 'mp'), may hold values from -0.15625 to 0.15625
- expert_up: bfloat16 [32, 768, 1536], P('seq', 'mp'), may hold values from -0.15625 to 0.15625
- expert_down: bfloat16 [32, 768, 1536], P('seq', 'mp'), may hold values from -0.21875 to 0.21875
Outputs:
- layer_out: bfloat16 [8192, 1536], P('seq', 'mp')
Inputs may be any that keep to these rules, and one draw needn't show every extreme that they name: `lengths`: sum to 8192; the longest is exactly 6144. `routes`: a token's 4 experts differ; among the rows of one device no expert is named more than 64 times, a bound that some block reaches.
All inputs are finite; a program needn't handle non-finite values.
Results may differ from a plain program's by a relative error of at most 0.018.
Values may be sent and summed in bfloat16 or wider, within the bound.
No kernel may reach another device: no remote copies, remote signals or barrier semaphores. Data moves between devices by JAX's collectives and lax.ppermute only.
A program may use at most 128 MiB of HBM per device.

v0:
```python
import math
import jax
import jax.numpy as jnp
from jax import lax
from jax.sharding import PartitionSpec as P

D = 1536
HQ = 12
KVH = 2
HD = 128
WINDOW = 4096
ROPE_BASE = 1500000.0
EPSILON = 1e-06


def prompt_ids(index, lengths):
    first_end = lengths[0]
    second_end = lengths[0] + lengths[1]
    prompt = (index >= first_end).astype(jnp.int32) + (index >= second_end).astype(jnp.int32)
    begin = jnp.where(index >= second_end, second_end, jnp.where(index >= first_end, first_end, 0))
    return (prompt, index - begin)


def rotary(values, position):
    half_dim = values.shape[-1] // 2
    freqs = jnp.exp(
        jnp.arange(half_dim, dtype=jnp.float32) * (-2.0 * math.log(ROPE_BASE) / values.shape[-1])
    )
    angles = position.astype(jnp.float32)[:, None] * freqs[None, :]
    cosine = jnp.cos(angles)[:, None, :]
    sine = jnp.sin(angles)[:, None, :]
    front = values[..., :half_dim]
    latter = values[..., half_dim:]
    return jnp.concatenate(
        [front * cosine - latter * sine, latter * cosine + front * sine], axis=-1
    )


def gather_seq(piece, count):
    rows = piece.shape[0]
    spread = jnp.broadcast_to(piece[None], (count,) + piece.shape).reshape(
        count * rows, piece.shape[1]
    )
    return lax.all_to_all(spread, "seq", 0, 0, tiled=True)


def local(
    hidden_in, wq, wkv, wo, lengths, routes, gate_logits, expert_gate, expert_up, expert_down
):
    tok_rows = hidden_in.shape[0]
    seq_index = lax.axis_index("seq")
    mp_index = lax.axis_index("mp")
    seq_count = lax.axis_size("seq")
    mp_count = lax.axis_size("mp")
    heads_here = wq.shape[1] // HD
    q_cols = heads_here * HD
    kv_group = mp_index * heads_here // (HQ // KVH)
    expert_all = lax.all_gather(
        jnp.concatenate([expert_gate, expert_up, expert_down], axis=0), "mp", axis=1, tiled=True
    )
    key_cols = lax.dynamic_slice_in_dim(wkv, kv_group * HD, HD, 1)
    value_cols = lax.dynamic_slice_in_dim(wkv, KVH * HD + kv_group * HD, HD, 1)
    piece = jnp.concatenate([wq, key_cols, value_cols, wo.T], axis=1)
    weights = gather_seq(piece, seq_count)
    w_qkv = weights[:, : q_cols + 2 * HD]
    wo_rows = weights[:, q_cols + 2 * HD :]
    whole = lax.all_gather(hidden_in, "mp", axis=1, tiled=True)
    whole_f = whole.astype(jnp.float32)
    normed = (
        whole_f * lax.rsqrt(jnp.sum(whole_f * whole_f, axis=-1, keepdims=True) / D + EPSILON)
    ).astype(jnp.bfloat16)
    lin = jnp.dot(normed, w_qkv, preferred_element_type=jnp.float32)
    own_index = seq_index * tok_rows + jnp.arange(tok_rows, dtype=jnp.int32)
    _, own_pos = prompt_ids(own_index, lengths)
    queries = (
        rotary(lin[:, :q_cols].reshape(tok_rows, heads_here, HD), own_pos)
        .astype(jnp.bfloat16)
        .transpose(1, 0, 2)
    )
    key_own = rotary(lin[:, q_cols : q_cols + HD].reshape(tok_rows, 1, HD), own_pos)[:, 0, :]
    value_own = lin[:, q_cols + HD :]
    kv_own = jnp.concatenate([key_own.astype(jnp.bfloat16), value_own.astype(jnp.bfloat16)], axis=1)
    back = min((WINDOW - 1 + tok_rows - 1) // tok_rows, seq_count - 1)
    blocks = []
    for k in range(back, 0, -1):
        blocks.append(lax.ppermute(kv_own, "seq", [(i, i + k) for i in range(seq_count - k)]))
    blocks.append(kv_own)
    kv_win = jnp.concatenate(blocks, axis=0)
    key_rows = kv_win[:, :HD]
    value_rows = kv_win[:, HD:].astype(jnp.float32)
    key_index = (seq_index - back) * tok_rows + jnp.arange((back + 1) * tok_rows, dtype=jnp.int32)
    scores = jnp.einsum(
        "hqd,kd->hqk", queries, key_rows, preferred_element_type=jnp.float32
    ) * HD ** (-0.5)
    query_prompt, _ = prompt_ids(own_index, lengths)
    key_prompt, _ = prompt_ids(key_index, lengths)
    spacing = own_index[:, None] - key_index[None, :]
    allowed = (
        (query_prompt[:, None] == key_prompt[None, :])
        & (spacing >= 0)
        & (spacing < WINDOW)
        & (key_index[None, :] >= 0)
    )[None]
    masked = jnp.where(allowed, scores, -1e30)
    peak = jnp.max(masked, axis=-1)
    probs = jnp.where(allowed, jnp.exp(masked - peak[..., None]), 0.0)
    total = jnp.sum(probs, axis=-1)
    accum = jnp.einsum("hqk,kd->hqd", probs, value_rows)
    attended = (
        (accum / total[..., None]).transpose(1, 0, 2).reshape(tok_rows, q_cols).astype(jnp.bfloat16)
    )
    partial_out = lax.dot_general(
        attended, wo_rows, (((1,), (1,)), ((), ())), preferred_element_type=jnp.float32
    )
    attn_mine = lax.psum_scatter(
        partial_out.astype(jnp.bfloat16), "mp", scatter_dimension=1, tiled=True
    ).astype(jnp.float32)
    residual = (hidden_in.astype(jnp.float32) + attn_mine).astype(jnp.bfloat16)
    residual_f = residual.astype(jnp.float32)
    square_sum = lax.psum(jnp.sum(residual_f * residual_f, axis=-1), "mp")
    moe_local = (residual_f * lax.rsqrt(square_sum / D + EPSILON)[:, None]).astype(jnp.bfloat16)
    local_experts = expert_gate.shape[0]
    experts = seq_count * local_experts
    top_count = routes.shape[1]
    capacity = 2 * tok_rows * top_count // experts
    part_cap = capacity // mp_count
    flat_ids = routes.reshape(-1)
    one_hot = (flat_ids[:, None] == jnp.arange(experts, dtype=jnp.int32)[None, :]).astype(jnp.int32)
    earlier_count = jnp.sum((jnp.cumsum(one_hot, axis=0) - one_hot) * one_hot, axis=1)
    mine = earlier_count // part_cap == mp_index
    slot_index = flat_ids * part_cap + earlier_count % part_cap
    send_index = jnp.where(mine, slot_index, experts * part_cap)
    source_row = jnp.arange(tok_rows * top_count, dtype=jnp.int32) // top_count
    full_rows = lax.all_gather(moe_local, "mp", axis=1, tiled=True)
    buffer = (
        jnp.zeros((experts * part_cap, D), jnp.bfloat16)
        .at[send_index]
        .set(full_rows[source_row], mode="drop")
    )
    arrived = lax.all_to_all(buffer, "seq", 0, 0, tiled=True)
    hidden_units = expert_all.shape[1]
    w_gate = expert_all[0]
    w_up = expert_all[1]
    w_down = expert_all[2]
    gate_act = lax.dot_general(
        arrived, w_gate, (((1,), (1,)), ((), ())), preferred_element_type=jnp.float32
    )
    up_act = lax.dot_general(
        arrived, w_up, (((1,), (1,)), ((), ())), preferred_element_type=jnp.float32
    )
    active = (jnp.maximum(gate_act, 0.0) * up_act).astype(jnp.bfloat16)
    result = jnp.dot(active, w_down, preferred_element_type=jnp.float32).astype(jnp.bfloat16)
    returned = lax.all_to_all(result, "seq", 0, 0, tiled=True)
    gate_weights = jax.nn.softmax(gate_logits, axis=-1)
    picked_back = returned[jnp.where(mine, slot_index, 0)].astype(jnp.float32)
    share = jnp.where(mine, gate_weights.reshape(-1), 0.0)
    weighted = picked_back * share[:, None]
    partial_moe = jnp.sum(weighted.reshape(tok_rows, top_count, D), axis=1)
    swapped = lax.all_to_all(partial_moe.astype(jnp.bfloat16), "mp", 1, 0, tiled=True)
    moe_total = jnp.sum(
        swapped.reshape(mp_count, tok_rows, D // mp_count).astype(jnp.float32), axis=0
    )
    del hidden_units
    return (residual_f + moe_total).astype(jnp.bfloat16)


def solution(mesh):
    return jax.shard_map(
        local,
        mesh=mesh,
        in_specs=(
            P("seq", "mp"),
            P("seq", "mp"),
            P("seq", None),
            P("mp", "seq"),
            P(),
            P("seq", None),
            P("seq", None),
            P("seq", "mp", None),
            P("seq", "mp", None),
            P("seq", "mp", None),
        ),
        out_specs=P("seq", "mp"),
        check_vma=False,
    )
```

profile of v0, /device:TPU:1, one launch (start us, length us, event | category | flops | bytes accessed | tf_op | source)
XLA Modules:
  0.0 351.0 jit_solution(2576738332656312989)
XLA Ops:
  8.1 2.0 broadcast_in_dim.38
  10.1 11.6 %all-to-all-start = ((bf16[32,48,1024]{2,1,0:T(8,128)(2,1)}), bf16[32,48,1024]{2,1,0:T(8,128)(2,1)}, u32[]{:S(2)}, u32[]{:S(2)}) async-start(bf16[32,48,1024]{2,1,0:T(8,128)(2,1)} %broadcast_in_dim.38), calls=%async_computation | async-start | bytes 6291456 | tf_op jit(solution)/shard_map/all_to_all | solution.py:44
  25.4 36.9 %all_gather.9 = bf16[256,1536]{1,0:T(8,128)(2,1)S(1)} all-gather(bf16[256,384]{1,0:T(8,128)(2,1)S(1)} %copy-done), channel_id=1, replica_groups=mesh['seq'=32,'mp'=4] {'mp'}, dimensions={1}, use_global_device_ids=true | all-gather | bytes 983040 | tf_op jit(solution)/shard_map/all_gather | solution.py:67
  63.1 1.6 fusion.10
  64.7 2.4 fusion.15
  67.6 5.4 %collective-permute-start = (bf16[256,256]{0,1:T(8,128)(2,1)S(1)}, bf16[256,256]{0,1:T(8,128)(2,1)}, u32[]{:S(2)}, u32[]{:S(2)}) collective-permute-start(bf16[256,256]{0,1:T(8,128)(2,1)S(1)} %pad_maximum_fusion.1), channel_id=1, source_target_pairs={{0,64},{4,68},{8,72},{12,76},{16,80},{20,84},{24,88},{28,92},{32,9... | collective-permute-start | bytes 393224 | tf_op jit(solution)/shard_map/ppermute | solution.py:86
  73.0 10.4 %collective-permute-start.1 = (bf16[256,256]{0,1:T(8,128)(2,1)S(1)}, bf16[256,256]{0,1:T(8,128)(2,1)}, u32[]{:S(2)}, u32[]{:S(2)}) collective-permute-start(bf16[256,256]{0,1:T(8,128)(2,1)S(1)} %pad_maximum_fusion.1), channel_id=1, source_target_pairs={{0,60},{4,64},{8,68},{12,72},{16,76},{20,80},{24,84},{28,88},{32,9... | collective-permute-start | bytes 393224 | tf_op jit(solution)/shard_map/ppermute | solution.py:86
  83.5 2.7 collective-permute-start.2
  86.2 1.9 collective-permute-start.3
  88.1 1.9 collective-permute-start.4
  90.8 1.3 collective-permute-start.5
  93.0 1.3 collective-permute-start.6
  94.3 0.9 constant_dynamic-update-slice_fusion.15
  95.2 1.3 collective-permute-start.7
  96.5 0.9 constant_dynamic-update-slice_fusion.14
  97.5 2.2 collective-permute-start.8
  99.7 0.9 constant_dynamic-update-slice_fusion.13
  100.6 5.7 %collective-permute-start.9 = (bf16[256,256]{0,1:T(8,128)(2,1)S(1)}, bf16[256,256]{0,1:T(8,128)(2,1)S(1)}, u32[]{:S(2)}, u32[]{:S(2)}) collective-permute-start(bf16[256,256]{0,1:T(8,128)(2,1)S(1)} %pad_maximum_fusion.1), channel_id=1, source_target_pairs={{0,28},{4,32},{8,36},{12,40},{16,44},{20,48},{24,52},{28,56},{32,6... | collective-permute-start | bytes 393224 | tf_op jit(solution)/shard_map/ppermute | solution.py:86
  106.3 0.9 constant_dynamic-update-slice_fusion.12
  107.3 1.3 collective-permute-start.10
  108.6 4.0 %collective-permute-start.11 = (bf16[256,256]{0,1:T(8,128)(2,1)S(1)}, bf16[256,256]{0,1:T(8,128)(2,1)S(1)}, u32[]{:S(2)}, u32[]{:S(2)}) collective-permute-start(bf16[256,256]{0,1:T(8,128)(2,1)S(1)} %pad_maximum_fusion.1), channel_id=1, source_target_pairs={{0,20},{4,24},{8,28},{12,32},{16,36},{20,40},{24,44},{28,48},{32,5... | collective-permute-start | bytes 393224 | tf_op jit(solution)/shard_map/ppermute | solution.py:86
  112.6 1.3 collective-permute-start.12
  113.9 4.6 %collective-permute-start.13 = (bf16[256,256]{0,1:T(8,128)(2,1)S(1)}, bf16[256,256]{0,1:T(8,128)(2,1)S(1)}, u32[]{:S(2)}, u32[]{:S(2)}) collective-permute-start(bf16[256,256]{0,1:T(8,128)(2,1)S(1)} %pad_maximum_fusion.1), channel_id=1, source_target_pairs={{0,12},{4,16},{8,20},{12,24},{16,28},{20,32},{24,36},{28,40},{32,4... | collective-permute-start | bytes 393224 | tf_op jit(solution)/shard_map/ppermute | solution.py:86
  118.6 1.7 collective-permute-start.14
  120.3 3.8 %collective-permute-start.15 = (bf16[256,256]{0,1:T(8,128)(2,1)S(1)}, bf16[256,256]{0,1:T(8,128)(2,1)S(1)}, u32[]{:S(2)}, u32[]{:S(2)}) collective-permute-start(bf16[256,256]{0,1:T(8,128)(2,1)S(1)} %pad_maximum_fusion.1), channel_id=1, source_target_pairs={{0,4},{4,8},{8,12},{12,16},{16,20},{20,24},{24,28},{28,32},{32,36}... | collective-permute-start | bytes 393224 | tf_op jit(solution)/shard_map/ppermute | solution.py:86
  124.2 2.3 collective-permute-done.15
  126.5 6.4 %fusion = (f32[3,256]{1,0:T(4,128)S(1)}, f32[3,256,4352]{2,1,0:T(8,128)}) fusion(pred[256,4352]{1,0:T(8,128)(4,1)S(1)} %fusion.10, bf16[4352,256]{0,1:T(8,128)(2,1)S(1)} %constant_dynamic-update-slice_fusion, bf16[256,3,64]{2,0,1:T(8,128)(2,1)S(1)} %get-tuple-element.9, bf16[256,3,64]{2,0,1:T(8,128)(2,1)S(1)} %get-tuple-element.8), kind=kOutput, calls=%fused_computation.5 | convolution fusion | flops 866057472 | bytes 15993856 | tf_op jit(solution)/shard_map/hqd,kd->hqk/dot_general | solution.py:92
  132.9 9.0 %fusion.1 = f32[3,256]{1,0:T(4,128)S(1)} fusion(f32[3,256,4352]{2,1,0:T(8,128)} %get-tuple-element.21, f32[3,256]{1,0:T(4,128)S(1)} %get-tuple-element.20, pred[256,4352]{1,0:T(8,128)(4,1)S(1)} %fusion.10), kind=kLoop, calls=%fused_computation.6 | loop fusion | flops 16710912 | bytes 14489600 | tf_op jit(solution)/shard_map/reduce_sum | solution.py:107
  141.9 6.9 %fusion.23 = bf16[256,3,128]{0,2,1:T(8,128)(2,1)S(1)} fusion(bf16[4352,256]{0,1:T(8,128)(2,1)S(1)} %constant_dynamic-update-slice_fusion, f32[3,256,4352]{2,1,0:T(8,128)} %get-tuple-element.21, f32[3,256]{1,0:T(4,128)S(1)} %get-tuple-element.20, pred[256,4352]{1,0:T(8,128)(4,1)S(1)} %fusion.10, f32[256,3]{0,1:T(4,128)S(1)} %bitcast.93), kind=kOutput, calls=%fused_computation.43 | convolution fusion | flops 869203968 | bytes 15802368 | tf_op jit(solution)/shard_map/hqk,kd->hqd/dot_general | solution.py:108
  148.8 2.0 convolution_convert_fusion.1
  150.9 1.2 copy.102
  152.2 1.5 pad_maximum_fusion
  154.2 9.0 %reduce-window.6 = s32[32,8,128]{2,1,0:T(8,128)S(1)} reduce-window(s32[32,8,128]{2,1,0:T(8,128)S(1)} %fusion.36, s32[]{:T(128)} %constant.82.clone.1), window={size=1x1x128 pad=0_0x0_0x127_0}, to_apply=%region_4.5 | reduce-window | flops 4161536 | bytes 262148 | tf_op jit(solution)/shard_map/reduce-window
  164.0 11.4 %reduce-scatter.4.cloned.1.call-done = bf16[384,256]{1,0:T(8,128)(2,1)} async-done(((bf16[1536,256]{1,0:T(8,128)(2,1)}), bf16[384,256]{1,0:T(8,128)(2,1)}) %reduce-scatter.4.cloned.1.call-update) | async-done | bytes 196624
  175.4 1.1 copy.103
  176.7 5.1 %psum.7 = f32[256]{0:T(256)S(1)} all-reduce(f32[256]{0:T(256)S(1)} %fusion.28), channel_id=1, replica_groups=mesh['seq'=32,'mp'=4] {'mp'}, use_global_device_ids=true, to_apply=%region_8.9 | all-reduce | flops 256 | bytes 2048 | tf_op jit(solution)/shard_map/psum | solution.py:120
  181.9 9.9 %all_gather.10 = bf16[256,1536]{1,0:T(8,128)(2,1)S(1)} all-gather(bf16[256,384]{1,0:T(8,128)(2,1)S(1)} %fusion.29), channel_id=1, replica_groups=mesh['seq'=32,'mp'=4] {'mp'}, dimensions={1}, use_global_device_ids=true | all-gather | bytes 983040 | tf_op jit(solution)/shard_map/all_gather | solution.py:134
  191.8 16.3 %scatter_custom_fusion = bf16[512,1536]{1,0:T(8,128)(2,1)S(1)} fusion(s32[1024]{0:T(1024)S(1)} %bitcast.94, bf16[256,1536]{1,0:T(8,128)(2,1)S(1)} %all_gather.10, s32[1024]{0:T(1024)S(1)} %broadcast_clamp_fusion.1, bf16[]{:T(256)} %constant.99.clone.1), kind=kCustom, calls=%fused_computation.19 | custom fusion | bytes 1572866 | tf_op jit(solution)/shard_map/scatter | solution.py:138
  208.1 35.9 %all_to_all.43 = bf16[32,16,1536]{2,1,0:T(8,128)(2,1)S(1)} all-to-all(bf16[32,16,1536]{2,1,0:T(8,128)(2,1)S(1)} %bitcast.79), channel_id=1, replica_groups=mesh['seq'=32,'mp'=4] {'seq'}, dimensions={0} | all-to-all | bytes 3145728 | tf_op jit(solution)/shard_map/all_to_all | solution.py:140
  244.1 21.3 %all-gather.2.cloned.1.call-done = bf16[3,768,1536]{2,1,0:T(8,128)(2,1)} async-done(((bf16[3,192,1536]{2,1,0:T(8,128)(2,1)}), bf16[3,768,1536]{2,1,0:T(8,128)(2,1)}) %all-gather.2.cloned.1.call-update) | async-done | bytes 7077904 | tf_op jit(solution)/shard_map/all_gather | solution.py:58
  265.3 3.1 fusion.13
  268.4 6.7 %convolution_convert_fusion = bf16[512,1536]{1,0:T(8,128)(2,1)} fusion(bf16[3,768,1536]{2,1,0:T(8,128)(2,1)} %all-gather.2.cloned.1.call-done, f32[512,768]{1,0:T(8,128)S(1)} %fusion.13, bf16[512,1536]{1,0:T(8,128)(2,1)S(1)} %bitcast.83), kind=kOutput, calls=%fused_computation.21 | convolution fusion | flops 2417885184 | bytes 9437184 | tf_op jit(solution)/shard_map/dot_general | solution.py:152
  275.2 9.2 %all-to-all-start.2 = ((bf16[32,16,1536]{2,1,0:T(8,128)(2,1)}), bf16[32,16,1536]{2,1,0:T(8,128)(2,1)S(1)}, u32[]{:S(2)}, u32[]{:S(2)}) async-start(bf16[32,16,1536]{2,1,0:T(8,128)(2,1)} %bitcast.23), calls=%async_computation.2 | async-start | bytes 3145728 | tf_op jit(solution)/shard_map/all_to_all | solution.py:153
  284.9 24.1 %all-to-all-done.2 = bf16[32,16,1536]{2,1,0:T(8,128)(2,1)S(1)} async-done(((bf16[32,16,1536]{2,1,0:T(8,128)(2,1)}), bf16[32,16,1536]{2,1,0:T(8,128)(2,1)S(1)}, u32[]{:S(2)}, u32[]{:S(2)}) %all-to-all-start.2) | async-done | bytes 1572896 | tf_op jit(solution)/shard_map/all_to_all | solution.py:153
  309.0 5.6 %gather_fusion = bf16[1024,1536]{1,0:T(8,128)(2,1)} fusion(bf16[512,1536]{1,0:T(8,128)(2,1)S(1)} %bitcast.78, s32[1024]{0:T(1024)S(1)} %broadcast_clamp_fusion), kind=kCustom, calls=%fused_computation.1 | custom fusion | bytes 6295552 | tf_op jit(solution)/shard_map/gather | solution.py:155
  314.7 6.7 %reshape.440 = f32[256,4,1536]{2,1,0:T(4,128)} reshape(bf16[1024,1536]{1,0:T(8,128)(2,1)} %gather_fusion) | data formatting | bytes 9437184 | tf_op jit(solution)/shard_map/convert_element_type | solution.py:155
  321.3 7.4 %multiply_reduce_fusion = bf16[256,1536]{1,0:T(8,128)(2,1)S(1)} fusion(f32[256,4,1536]{2,1,0:T(4,128)} %reshape.440, f32[256,4]{1,0:T(8,128)S(1)} %copy.97), kind=kLoop, calls=%fused_computation.15 | loop fusion | flops 2752512 | bytes 7081984 | tf_op jit(solution)/shard_map/reduce_sum | solution.py:158
  329.4 13.7 %all_to_all.44 = bf16[256,4,384]{2,0,1:T(8,128)(2,1)S(1)} all-to-all(bf16[256,4,384]{2,0,1:T(8,128)(2,1)S(1)} %copy.99), channel_id=1, replica_groups=mesh['seq'=32,'mp'=4] {'mp'}, dimensions={1} | all-to-all | bytes 1572864 | tf_op jit(solution)/shard_map/all_to_all | solution.py:159
  (103 shorter events, 10.4 us)
Async XLA Ops:
  10.1 11.7 %copy-start.6 = (s32[3]{0:T(128)S(1)}, s32[3]{0:T(128)}, u32[]{:S(2)}) copy-start(s32[3]{0:T(128)} %param.14) | copy-start | bytes 40
  10.1 15.3 %copy-start = (bf16[256,384]{1,0:T(8,128)(2,1)S(1)}, bf16[256,384]{1,0:T(8,128)(2,1)}, u32[]{:S(2)}) copy-start(bf16[256,384]{1,0:T(8,128)(2,1)} %param.10) | copy-start | bytes 589828
  10.1 54.5 %all-to-all-start = ((bf16[32,48,1024]{2,1,0:T(8,128)(2,1)}), bf16[32,48,1024]{2,1,0:T(8,128)(2,1)}, u32[]{:S(2)}, u32[]{:S(2)}) async-start(bf16[32,48,1024]{2,1,0:T(8,128)(2,1)} %broadcast_in_dim.38), calls=%async_computation | async-start | bytes 6291456 | tf_op jit(solution)/shard_map/all_to_all | solution.py:44
  21.7 153.7 %reduce-scatter.4.cloned.1.call-start = ((), (), s32[]{:S(2)}) async-start(), calls=%async_computation.6 | async-start | bytes 983040
  67.6 23.1 %collective-permute-start = (bf16[256,256]{0,1:T(8,128)(2,1)S(1)}, bf16[256,256]{0,1:T(8,128)(2,1)}, u32[]{:S(2)}, u32[]{:S(2)}) collective-permute-start(bf16[256,256]{0,1:T(8,128)(2,1)S(1)} %pad_maximum_fusion.1), channel_id=1, source_target_pairs={{0,64},{4,68},{8,72},{12,76},{16,80},{20,84},{24,88},{28,92},{32,9... | collective-permute-start | bytes 393224 | tf_op jit(solution)/shard_map/ppermute | solution.py:86
  73.0 20.0 %collective-permute-start.1 = (bf16[256,256]{0,1:T(8,128)(2,1)S(1)}, bf16[256,256]{0,1:T(8,128)(2,1)}, u32[]{:S(2)}, u32[]{:S(2)}) collective-permute-start(bf16[256,256]{0,1:T(8,128)(2,1)S(1)} %pad_maximum_fusion.1), channel_id=1, source_target_pairs={{0,60},{4,64},{8,68},{12,72},{16,76},{20,80},{24,84},{28,88},{32,9... | collective-permute-start | bytes 393224 | tf_op jit(solution)/shard_map/ppermute | solution.py:86
  83.5 11.7 %collective-permute-start.2 = (bf16[256,256]{0,1:T(8,128)(2,1)S(1)}, bf16[256,256]{0,1:T(8,128)(2,1)}, u32[]{:S(2)}, u32[]{:S(2)}) collective-permute-start(bf16[256,256]{0,1:T(8,128)(2,1)S(1)} %pad_maximum_fusion.1), channel_id=1, source_target_pairs={{0,56},{4,60},{8,64},{12,68},{16,72},{20,76},{24,80},{28,84},{32,8... | collective-permute-start | bytes 393224 | tf_op jit(solution)/shard_map/ppermute | solution.py:86
  86.2 11.3 %collective-permute-start.3 = (bf16[256,256]{0,1:T(8,128)(2,1)S(1)}, bf16[256,256]{0,1:T(8,128)(2,1)}, u32[]{:S(2)}, u32[]{:S(2)}) collective-permute-start(bf16[256,256]{0,1:T(8,128)(2,1)S(1)} %pad_maximum_fusion.1), channel_id=1, source_target_pairs={{0,52},{4,56},{8,60},{12,64},{16,68},{20,72},{24,76},{28,80},{32,8... | collective-permute-start | bytes 393224 | tf_op jit(solution)/shard_map/ppermute | solution.py:86
  88.1 12.5 %collective-permute-start.4 = (bf16[256,256]{0,1:T(8,128)(2,1)S(1)}, bf16[256,256]{0,1:T(8,128)(2,1)}, u32[]{:S(2)}, u32[]{:S(2)}) collective-permute-start(bf16[256,256]{0,1:T(8,128)(2,1)S(1)} %pad_maximum_fusion.1), channel_id=1, source_target_pairs={{0,48},{4,52},{8,56},{12,60},{16,64},{20,68},{24,72},{28,76},{32,8... | collective-permute-start | bytes 393224 | tf_op jit(solution)/shard_map/ppermute | solution.py:86
  90.8 16.5 %collective-permute-start.5 = (bf16[256,256]{0,1:T(8,128)(2,1)S(1)}, bf16[256,256]{0,1:T(8,128)(2,1)S(1)}, u32[]{:S(2)}, u32[]{:S(2)}) collective-permute-start(bf16[256,256]{0,1:T(8,128)(2,1)S(1)} %pad_maximum_fusion.1), channel_id=1, source_target_pairs={{0,44},{4,48},{8,52},{12,56},{16,60},{20,64},{24,68},{28,72},{32,7... | collective-permute-start | bytes 393224 | tf_op jit(solution)/shard_map/ppermute | solution.py:86
  93.0 15.6 %collective-permute-start.6 = (bf16[256,256]{0,1:T(8,128)(2,1)S(1)}, bf16[256,256]{0,1:T(8,128)(2,1)S(1)}, u32[]{:S(2)}, u32[]{:S(2)}) collective-permute-start(bf16[256,256]{0,1:T(8,128)(2,1)S(1)} %pad_maximum_fusion.1), channel_id=1, source_target_pairs={{0,40},{4,44},{8,48},{12,52},{16,56},{20,60},{24,64},{28,68},{32,7... | collective-permute-start | bytes 393224 | tf_op jit(solution)/shard_map/ppermute | solution.py:86
  95.2 17.3 %collective-permute-start.7 = (bf16[256,256]{0,1:T(8,128)(2,1)S(1)}, bf16[256,256]{0,1:T(8,128)(2,1)S(1)}, u32[]{:S(2)}, u32[]{:S(2)}) collective-permute-start(bf16[256,256]{0,1:T(8,128)(2,1)S(1)} %pad_maximum_fusion.1), channel_id=1, source_target_pairs={{0,36},{4,40},{8,44},{12,48},{16,52},{20,56},{24,60},{28,64},{32,6... | collective-permute-start | bytes 393224 | tf_op jit(solution)/shard_map/ppermute | solution.py:86
  97.5 16.5 %collective-permute-start.8 = (bf16[256,256]{0,1:T(8,128)(2,1)S(1)}, bf16[256,256]{0,1:T(8,128)(2,1)S(1)}, u32[]{:S(2)}, u32[]{:S(2)}) collective-permute-start(bf16[256,256]{0,1:T(8,128)(2,1)S(1)} %pad_maximum_fusion.1), channel_id=1, source_target_pairs={{0,32},{4,36},{8,40},{12,44},{16,48},{20,52},{24,56},{28,60},{32,6... | collective-permute-start | bytes 393224 | tf_op jit(solution)/shard_map/ppermute | solution.py:86
  100.6 18.0 %collective-permute-start.9 = (bf16[256,256]{0,1:T(8,128)(2,1)S(1)}, bf16[256,256]{0,1:T(8,128)(2,1)S(1)}, u32[]{:S(2)}, u32[]{:S(2)}) collective-permute-start(bf16[256,256]{0,1:T(8,128)(2,1)S(1)} %pad_maximum_fusion.1), channel_id=1, source_target_pairs={{0,28},{4,32},{8,36},{12,40},{16,44},{20,48},{24,52},{28,56},{32,6... | collective-permute-start | bytes 393224 | tf_op jit(solution)/shard_map/ppermute | solution.py:86
  107.3 13.0 %collective-permute-start.10 = (bf16[256,256]{0,1:T(8,128)(2,1)S(1)}, bf16[256,256]{0,1:T(8,128)(2,1)S(1)}, u32[]{:S(2)}, u32[]{:S(2)}) collective-permute-start(bf16[256,256]{0,1:T(8,128)(2,1)S(1)} %pad_maximum_fusion.1), channel_id=1, source_target_pairs={{0,24},{4,28},{8,32},{12,36},{16,40},{20,44},{24,48},{28,52},{32,5... | collective-permute-start | bytes 393224 | tf_op jit(solution)/shard_map/ppermute | solution.py:86
  108.6 15.5 %collective-permute-start.11 = (bf16[256,256]{0,1:T(8,128)(2,1)S(1)}, bf16[256,256]{0,1:T(8,128)(2,1)S(1)}, u32[]{:S(2)}, u32[]{:S(2)}) collective-permute-start(bf16[256,256]{0,1:T(8,128)(2,1)S(1)} %pad_maximum_fusion.1), channel_id=1, source_target_pairs={{0,20},{4,24},{8,28},{12,32},{16,36},{20,40},{24,44},{28,48},{32,5... | collective-permute-start | bytes 393224 | tf_op jit(solution)/shard_map/ppermute | solution.py:86
  112.6 11.5 %collective-permute-start.12 = (bf16[256,256]{0,1:T(8,128)(2,1)S(1)}, bf16[256,256]{0,1:T(8,128)(2,1)S(1)}, u32[]{:S(2)}, u32[]{:S(2)}) collective-permute-start(bf16[256,256]{0,1:T(8,128)(2,1)S(1)} %pad_maximum_fusion.1), channel_id=1, source_target_pairs={{0,16},{4,20},{8,24},{12,28},{16,32},{20,36},{24,40},{28,44},{32,4... | collective-permute-start | bytes 393224 | tf_op jit(solution)/shard_map/ppermute | solution.py:86
  113.9 10.2 %collective-permute-start.13 = (bf16[256,256]{0,1:T(8,128)(2,1)S(1)}, bf16[256,256]{0,1:T(8,128)(2,1)S(1)}, u32[]{:S(2)}, u32[]{:S(2)}) collective-permute-start(bf16[256,256]{0,1:T(8,128)(2,1)S(1)} %pad_maximum_fusion.1), channel_id=1, source_target_pairs={{0,12},{4,16},{8,20},{12,24},{16,28},{20,32},{24,36},{28,40},{32,4... | collective-permute-start | bytes 393224 | tf_op jit(solution)/shard_map/ppermute | solution.py:86
  118.6 5.6 %collective-permute-start.14 = (bf16[256,256]{0,1:T(8,128)(2,1)S(1)}, bf16[256,256]{0,1:T(8,128)(2,1)S(1)}, u32[]{:S(2)}, u32[]{:S(2)}) collective-permute-start(bf16[256,256]{0,1:T(8,128)(2,1)S(1)} %pad_maximum_fusion.1), channel_id=1, source_target_pairs={{0,8},{4,12},{8,16},{12,20},{16,24},{20,28},{24,32},{28,36},{32,40... | collective-permute-start | bytes 393224 | tf_op jit(solution)/shard_map/ppermute | solution.py:86
  120.3 6.2 %collective-permute-start.15 = (bf16[256,256]{0,1:T(8,128)(2,1)S(1)}, bf16[256,256]{0,1:T(8,128)(2,1)S(1)}, u32[]{:S(2)}, u32[]{:S(2)}) collective-permute-start(bf16[256,256]{0,1:T(8,128)(2,1)S(1)} %pad_maximum_fusion.1), channel_id=1, source_target_pairs={{0,4},{4,8},{8,12},{12,16},{16,20},{20,24},{24,28},{28,32},{32,36}... | collective-permute-start | bytes 393224 | tf_op jit(solution)/shard_map/ppermute | solution.py:86
  148.8 3.4 copy-start.1
  148.8 3.4 copy-start.2
  148.8 3.4 copy-start.3
  152.1 1.6 copy-start.5
  152.2 113.2 %all-gather.2.cloned.1.call-start = ((), (), s32[]{:S(2)}) async-start(), calls=%async_computation.5 | async-start | bytes 8847360 | tf_op jit(solution)/shard_map/all_gather | solution.py:58
  275.2 9.5 %copy-start.4 = (f32[256,4]{0,1:T(4,128)S(1)}, f32[256,4]{0,1:T(4,128)}, u32[]{:S(2)}) copy-start(f32[256,4]{0,1:T(4,128)} %param.16) | copy-start | bytes 12292
  275.2 33.8 %all-to-all-start.2 = ((bf16[32,16,1536]{2,1,0:T(8,128)(2,1)}), bf16[32,16,1536]{2,1,0:T(8,128)(2,1)S(1)}, u32[]{:S(2)}, u32[]{:S(2)}) async-start(bf16[32,16,1536]{2,1,0:T(8,128)(2,1)} %bitcast.23), calls=%async_computation.2 | async-start | bytes 3145728 | tf_op jit(solution)/shard_map/all_to_all | solution.py:153
Sparse Core Ops, SparseCore 0:
  152.3 23.1 reduce-scatter.3
  177.1 88.1 all-gather.1
where the time goes:
time: 357 us; the launch traced here: 351 us
  blocking collectives  101 us (28%)
  starting transfers between devices  71.8 us (20%)
  waiting for transfers between devices  59.2 us (17%)
  local copies, waits for them, and re-layouts  41.8 us (12%)
  other arithmetic  33.7 us (9%)
  matrix products  27.5 us (8%)
  between operations  15.6 us (4%)
    ppermute x16, starting transfers between devices, local(): lax.ppermute(kv_own, 'seq', [(i, i + k) for i in range(seq_count - k)])  50.9 us
    all_gather x1, blocking collectives, local(): whole = lax.all_gather(hidden_in, 'mp', axis=1, tiled=True)  36.9 us
    all_to_all x1, blocking collectives, local(): arrived = lax.all_to_all(buffer, 'seq', 0, 0, tiled=True)  35.9 us
    all_to_all x1, waiting for transfers between devices, local(): returned = lax.all_to_all(result, 'seq', 0, 0, tiled=True)  24.1 us
    all_gather x1, waiting for transfers between devices, local(): lax.all_gather(jnp.concatenate([expert_gate, expert_up, expert_down], axi...  21.3 us
    scatter x1, local copies, waits for them, and re-layouts, local(): buffer = jnp.zeros((experts * part_cap, D), jnp.bfloat16).at[send_index]....  16.3 us
    all_to_all x1, blocking collectives, local(): lax.all_to_all(partial_moe.astype(jnp.bfloat16), 'mp', 1, 0, tiled=True)  13.7 us
    all_to_all x1, starting transfers between devices, gather_seq(): return lax.all_to_all(spread, 'seq', 0, 0, tiled=True)  11.6 us
  transfers between devices with their start and end apart: 20, of which 4 were waited for; matrix products, arithmetic and copies ran while one was open for 11% of the time, Pallas kernels for 0%

commit v1 on v0

--- a/solution.py
+++ b/solution.py
@@ -55,9 +55,9 @@
     heads_here = wq.shape[1] // HD
     q_cols = heads_here * HD
     kv_group = mp_index * heads_here // (HQ // KVH)
-    expert_all = lax.all_gather(
-        jnp.concatenate([expert_gate, expert_up, expert_down], axis=0), "mp", axis=1, tiled=True
-    )
+    own = jnp.concatenate([expert_gate, expert_up, expert_down], axis=0)
+    sent = jnp.stack([own] * lax.axis_size("mp"))
+    expert_all = jnp.concatenate(lax.all_to_all(sent, "mp", 0, 0), axis=1)
     key_cols = lax.dynamic_slice_in_dim(wkv, kv_group * HD, HD, 1)
     value_cols = lax.dynamic_slice_in_dim(wkv, KVH * HD + kv_group * HD, HD, 1)
     piece = jnp.concatenate([wq, key_cols, value_cols, wo.T], axis=1)

time: 357 us -> 384 us (1.076)
  waiting for transfers between devices: 59.2 us -> 97.5 us
  blocking collectives: 101 us -> 66.8 us
  local copies, waits for them, and re-layouts: 41.8 us -> 52.7 us
  starting transfers between devices: 71.8 us -> 80.8 us
    all_to_all x1 -> x0, blocking collectives: 35.9 us -> none  [local(): arrived = lax.all_to_all(buffer, 'seq', 0, 0, tiled=True)]
    ppermute x16, waiting for transfers between devices: 2.31 us -> 30.7 us  [local(): lax.ppermute(kv_own, 'seq', [(i, i + k) for i in range(seq_count - k)])]
    all_gather x1 -> x0, waiting for transfers between devices: 21.3 us -> none  [local(): lax.all_gather(jnp.concatenate([expert_gate, expert_up, expert_down], axi...]
    unnamed x3 -> x2, waiting for transfers between devices: 11.4 us -> 29.1 us
    all_to_all x0 -> x2, waiting for transfers between devices: none -> 16.9 us  [the longest x1 16.9 us: local(): arrived = lax.all_to_all(buffer, 'seq', 0, 0, tiled=True)]
    all_to_all x0 -> x2, starting transfers between devices: none -> 14.9 us  [the longest x1 9.33 us: local(): arrived = lax.all_to_all(buffer, 'seq', 0, 0, tiled=True)]
    slice x2 -> x3, local copies, waits for them, and re-layouts: 0.22 us -> 6.32 us  [the longest x1 6.1 us: local(): w_up = expert_all[1]]
  transfers between devices with their start and end apart: 20 -> 21, of which waited for: 4 -> 7; matrix products, arithmetic and copies ran while one was open for 11% -> 20% of each run, Pallas kernels for 0% -> 0%
where the time goes in v1:
time: 384 us; the launch traced here: 377 us
  waiting for transfers between devices  97.5 us (25%)
  starting transfers between devices  80.8 us (21%)
  blocking collectives  66.8 us (17%)
  local copies, waits for them, and re-layouts  52.7 us (14%)
  other arithmetic  34 us (9%)
  matrix products  29 us (8%)
  between operations  15.6 us (4%)
    ppermute x16, starting transfers between devices, local(): lax.ppermute(kv_own, 'seq', [(i, i + k) for i in range(seq_count - k)])  48.8 us
    all_gather x1, blocking collectives, local(): whole = lax.all_gather(hidden_in, 'mp', axis=1, tiled=True)  36.2 us
    ppermute x16, waiting for transfers between devices, local(): lax.ppermute(kv_own, 'seq', [(i, i + k) for i in range(seq_count - k)])  30.7 us
    unnamed x2, waiting for transfers between devices  29.1 us
    all_to_all x1, waiting for transfers between devices, local(): returned = lax.all_to_all(result, 'seq', 0, 0, tiled=True)  20.9 us
    scatter x1, local copies, waits for them, and re-layouts, local(): buffer = jnp.zeros((experts * part_cap, D), jnp.bfloat16).at[send_index]....  17.2 us
    all_to_all x1, waiting for transfers between devices, local(): arrived = lax.all_to_all(buffer, 'seq', 0, 0, tiled=True)  16.9 us
    all_to_all x1, blocking collectives, local(): lax.all_to_all(partial_moe.astype(jnp.bfloat16), 'mp', 1, 0, tiled=True)  15.7 us
  transfers between devices with their start and end apart: 21, of which 7 were waited for; matrix products, arithmetic and copies ran while one was open for 20% of the time, Pallas kernels for 0%

profile of v1, /device:TPU:1, one launch (start us, length us, event | category | flops | bytes accessed | tf_op | source)
XLA Modules:
  0.0 376.5 jit_solution(5798769173820752925)
XLA Ops:
  8.1 2.0 broadcast_in_dim.38
  10.1 11.6 %all-to-all-start = ((bf16[32,48,1024]{2,1,0:T(8,128)(2,1)}), bf16[32,48,1024]{2,1,0:T(8,128)(2,1)}, u32[]{:S(2)}, u32[]{:S(2)}) async-start(bf16[32,48,1024]{2,1,0:T(8,128)(2,1)} %broadcast_in_dim.38), calls=%async_computation | async-start | bytes 6291456 | tf_op jit(solution)/shard_map/all_to_all | solution.py:44
  26.1 36.2 %all_gather.6 = bf16[256,1536]{1,0:T(8,128)(2,1)S(1)} all-gather(bf16[256,384]{1,0:T(8,128)(2,1)S(1)} %copy-done.2), channel_id=1, replica_groups=mesh['seq'=32,'mp'=4] {'mp'}, dimensions={1}, use_global_device_ids=true | all-gather | bytes 983040 | tf_op jit(solution)/shard_map/all_gather | solution.py:67
  63.7 1.4 pad_maximum_fusion
  65.1 1.6 fusion.10
  66.7 3.5 stack.2
  70.3 5.6 %all-to-all-start.2 = ((bf16[4,3,192,1536]{3,2,1,0:T(8,128)(2,1)}), bf16[4,3,192,1536]{3,2,1,0:T(8,128)(2,1)}, u32[]{:S(2)}, u32[]{:S(2)}) async-start(bf16[4,3,192,1536]{3,2,1,0:T(8,128)(2,1)} %stack.2), calls=%async_computation.2 | async-start | bytes 14155776 | tf_op jit(solution)/shard_map/all_to_all | solution.py:60
  75.9 2.4 fusion.13
  78.9 5.4 %collective-permute-start = (bf16[256,256]{0,1:T(8,128)(2,1)S(1)}, bf16[256,256]{0,1:T(8,128)(2,1)}, u32[]{:S(2)}, u32[]{:S(2)}) collective-permute-start(bf16[256,256]{0,1:T(8,128)(2,1)S(1)} %pad_maximum_fusion.1), channel_id=1, source_target_pairs={{0,64},{4,68},{8,72},{12,76},{16,80},{20,84},{24,88},{28,92},{32,9... | collective-permute-start | bytes 393224 | tf_op jit(solution)/shard_map/ppermute | solution.py:86
  84.3 10.5 %collective-permute-start.1 = (bf16[256,256]{0,1:T(8,128)(2,1)S(1)}, bf16[256,256]{0,1:T(8,128)(2,1)}, u32[]{:S(2)}, u32[]{:S(2)}) collective-permute-start(bf16[256,256]{0,1:T(8,128)(2,1)S(1)} %pad_maximum_fusion.1), channel_id=1, source_target_pairs={{0,60},{4,64},{8,68},{12,72},{16,76},{20,80},{24,84},{28,88},{32,9... | collective-permute-start | bytes 393224 | tf_op jit(solution)/shard_map/ppermute | solution.py:86
  94.7 2.7 collective-permute-start.2
  97.4 2.0 collective-permute-start.3
  99.4 1.9 collective-permute-start.4
  102.0 1.3 collective-permute-start.5
  104.3 1.3 collective-permute-start.6
  106.5 1.3 collective-permute-start.7
  108.7 2.4 collective-permute-start.8
  112.1 5.5 %collective-permute-start.9 = (bf16[256,256]{0,1:T(8,128)(2,1)S(1)}, bf16[256,256]{0,1:T(8,128)(2,1)S(1)}, u32[]{:S(2)}, u32[]{:S(2)}) collective-permute-start(bf16[256,256]{0,1:T(8,128)(2,1)S(1)} %pad_maximum_fusion.1), channel_id=1, source_target_pairs={{0,28},{4,32},{8,36},{12,40},{16,44},{20,48},{24,52},{28,56},{32,6... | collective-permute-start | bytes 393224 | tf_op jit(solution)/shard_map/ppermute | solution.py:86
  118.5 1.3 collective-permute-start.10
  119.8 4.2 %collective-permute-start.11 = (bf16[256,256]{0,1:T(8,128)(2,1)S(1)}, bf16[256,256]{0,1:T(8,128)(2,1)S(1)}, u32[]{:S(2)}, u32[]{:S(2)}) collective-permute-start(bf16[256,256]{0,1:T(8,128)(2,1)S(1)} %pad_maximum_fusion.1), channel_id=1, source_target_pairs={{0,20},{4,24},{8,28},{12,32},{16,36},{20,40},{24,44},{28,48},{32,5... | collective-permute-start | bytes 393224 | tf_op jit(solution)/shard_map/ppermute | solution.py:86
  124.1 1.3 collective-permute-start.12
  125.5 4.6 %collective-permute-start.13 = (bf16[256,256]{0,1:T(8,128)(2,1)S(1)}, bf16[256,256]{0,1:T(8,128)(2,1)S(1)}, u32[]{:S(2)}, u32[]{:S(2)}) collective-permute-start(bf16[256,256]{0,1:T(8,128)(2,1)S(1)} %pad_maximum_fusion.1), channel_id=1, source_target_pairs={{0,12},{4,16},{8,20},{12,24},{16,28},{20,32},{24,36},{28,40},{32,4... | collective-permute-start | bytes 393224 | tf_op jit(solution)/shard_map/ppermute | solution.py:86
  130.1 24.9 %collective-permute-done.9 = bf16[256,256]{0,1:T(8,128)(2,1)S(1)} collective-permute-done((bf16[256,256]{0,1:T(8,128)(2,1)S(1)}, bf16[256,256]{0,1:T(8,128)(2,1)S(1)}, u32[]{:S(2)}, u32[]{:S(2)}) %collective-permute-start.9) | collective-permute-done | bytes 131104 | tf_op jit(solution)/shard_map/ppermute | solution.py:86
  155.0 1.3 collective-permute-start.14
  156.3 1.5 collective-permute-done.10
  157.8 1.8 collective-permute-start.15
  159.6 1.4 collective-permute-done.11
  161.1 2.8 collective-permute-done.12
  164.0 6.4 %fusion = (f32[3,256]{1,0:T(4,128)S(1)}, f32[3,256,4352]{2,1,0:T(8,128)}) fusion(pred[256,4352]{1,0:T(8,128)(4,1)S(1)} %fusion.10, bf16[4352,256]{0,1:T(8,128)(2,1)S(1)} %constant_dynamic-update-slice_fusion, bf16[256,3,64]{2,0,1:T(8,128)(2,1)S(1)} %get-tuple-element.12, bf16[256,3,64]{2,0,1:T(8,128)(2,1)S(1)} %get-tuple-element.11), kind=kOutput, calls=%fused_computation.5 | convolution fusion | flops 866057472 | bytes 15993856 | tf_op jit(solution)/shard_map/hqd,kd->hqk/dot_general | solution.py:92
  170.4 9.0 %fusion.1 = f32[3,256]{1,0:T(4,128)S(1)} fusion(f32[3,256,4352]{2,1,0:T(8,128)} %get-tuple-element.24, f32[3,256]{1,0:T(4,128)S(1)} %get-tuple-element.23, pred[256,4352]{1,0:T(8,128)(4,1)S(1)} %fusion.10), kind=kLoop, calls=%fused_computation.6 | loop fusion | flops 16710912 | bytes 14489600 | tf_op jit(solution)/shard_map/reduce_sum | solution.py:107
  179.4 6.9 %fusion.21 = bf16[256,3,128]{0,2,1:T(8,128)(2,1)S(1)} fusion(bf16[4352,256]{0,1:T(8,128)(2,1)S(1)} %constant_dynamic-update-slice_fusion, f32[3,256,4352]{2,1,0:T(8,128)} %get-tuple-element.24, f32[3,256]{1,0:T(4,128)S(1)} %get-tuple-element.23, pred[256,4352]{1,0:T(8,128)(4,1)S(1)} %fusion.10, f32[256,3]{0,1:T(4,128)S(1)} %bitcast.90), kind=kOutput, calls=%fused_computation.38 | convolution fusion | flops 869203968 | bytes 15802368 | tf_op jit(solution)/shard_map/hqk,kd->hqd/dot_general | solution.py:108
  186.3 1.9 convolution_convert_fusion.1
  189.4 9.0 %reduce-window.6 = s32[32,8,128]{2,1,0:T(8,128)S(1)} reduce-window(s32[32,8,128]{2,1,0:T(8,128)S(1)} %fusion.33, s32[]{:T(128)} %constant.82.clone.1), window={size=1x1x128 pad=0_0x0_0x127_0}, to_apply=%region_4.5 | reduce-window | flops 4161536 | bytes 262148 | tf_op jit(solution)/shard_map/reduce-window
  199.3 29.1 %reduce-scatter.4.cloned.1.call-done = bf16[384,256]{1,0:T(8,128)(2,1)} async-done(((bf16[1536,256]{1,0:T(8,128)(2,1)}), bf16[384,256]{1,0:T(8,128)(2,1)}) %reduce-scatter.4.cloned.1.call-update) | async-done | bytes 196624
  229.6 5.3 %psum.7 = f32[256]{0:T(256)S(1)} all-reduce(f32[256]{0:T(256)S(1)} %fusion.25), channel_id=1, replica_groups=mesh['seq'=32,'mp'=4] {'mp'}, use_global_device_ids=true, to_apply=%region_8.9 | all-reduce | flops 256 | bytes 2048 | tf_op jit(solution)/shard_map/psum | solution.py:120
  235.1 9.6 %all_gather.7 = bf16[256,1536]{1,0:T(8,128)(2,1)S(1)} all-gather(bf16[256,384]{1,0:T(8,128)(2,1)S(1)} %fusion.26), channel_id=1, replica_groups=mesh['seq'=32,'mp'=4] {'mp'}, dimensions={1}, use_global_device_ids=true | all-gather | bytes 983040 | tf_op jit(solution)/shard_map/all_gather | solution.py:134
  244.7 17.2 %scatter_custom_fusion = bf16[512,1536]{1,0:T(8,128)(2,1)} fusion(s32[1024]{0:T(1024)S(1)} %bitcast.91, bf16[256,1536]{1,0:T(8,128)(2,1)S(1)} %all_gather.7, s32[1024]{0:T(1024)S(1)} %broadcast_clamp_fusion.1, bf16[]{:T(256)} %constant.99.clone.1), kind=kCustom, calls=%fused_computation.19 | custom fusion | bytes 1572866 | tf_op jit(solution)/shard_map/scatter | solution.py:138
  261.9 9.3 %all-to-all-start.1 = ((bf16[32,16,1536]{2,1,0:T(8,128)(2,1)}), bf16[32,16,1536]{2,1,0:T(8,128)(2,1)S(1)}, u32[]{:S(2)}, u32[]{:S(2)}) async-start(bf16[32,16,1536]{2,1,0:T(8,128)(2,1)} %bitcast.18), calls=%async_computation.1 | async-start | bytes 3145728 | tf_op jit(solution)/shard_map/all_to_all | solution.py:140
  271.2 6.1 %fusion.58 = (bf16[1,4,192,1536]{3,2,0,1:T(8,128)(2,1)}, bf16[1,4,192,1536]{3,2,0,1:T(8,128)(2,1)}, bf16[1,4,192,1536]{3,2,0,1:T(8,128)(2,1)}) fusion(bf16[3,4,192,1536]{3,2,0,1:T(8,128)(2,1)} %bitcast.20), kind=kLoop, calls=%fused_computation.142 | loop fusion | bytes 14155776 | tf_op jit(solution)/shard_map/slice | solution.py:143
  277.3 16.9 %all-to-all-done.1 = bf16[32,16,1536]{2,1,0:T(8,128)(2,1)S(1)} async-done(((bf16[32,16,1536]{2,1,0:T(8,128)(2,1)}), bf16[32,16,1536]{2,1,0:T(8,128)(2,1)S(1)}, u32[]{:S(2)}, u32[]{:S(2)}) %all-to-all-start.1) | async-done | bytes 1572896 | tf_op jit(solution)/shard_map/all_to_all | solution.py:140
  294.2 4.3 %fusion.61 = f32[512,768]{1,0:T(8,128)} fusion(bf16[512,1536]{1,0:T(8,128)(2,1)S(1)} %bitcast.79, bf16[768,1536]{1,0:T(8,128)(2,1)} %bitcast.77), kind=kOutput, calls=%fused_computation.145 | convolution fusion | flops 1207959552 | bytes 5505024 | tf_op jit(solution)/shard_map/dot_general | solution.py:145
  298.5 7.2 %convolution_convert_fusion = bf16[512,1536]{1,0:T(8,128)(2,1)} fusion(bf16[768,1536]{1,0:T(8,128)(2,1)} %bitcast.76, f32[512,768]{1,0:T(8,128)} %fusion.61, bf16[512,1536]{1,0:T(8,128)(2,1)S(1)} %bitcast.80, bf16[768,1536]{1,0:T(8,128)(2,1)} %bitcast.75), kind=kOutput, calls=%fused_computation.21 | convolution fusion | flops 2417885184 | bytes 9437184 | tf_op jit(solution)/shard_map/dot_general | solution.py:152
  305.7 5.5 %all-to-all-start.3 = ((bf16[32,16,1536]{2,1,0:T(8,128)(2,1)}), bf16[32,16,1536]{2,1,0:T(8,128)(2,1)S(1)}, u32[]{:S(2)}, u32[]{:S(2)}) async-start(bf16[32,16,1536]{2,1,0:T(8,128)(2,1)} %bitcast.78), calls=%async_computation.3 | async-start | bytes 3145728 | tf_op jit(solution)/shard_map/all_to_all | solution.py:153
  311.7 20.9 %all-to-all-done.3 = bf16[32,16,1536]{2,1,0:T(8,128)(2,1)S(1)} async-done(((bf16[32,16,1536]{2,1,0:T(8,128)(2,1)}), bf16[32,16,1536]{2,1,0:T(8,128)(2,1)S(1)}, u32[]{:S(2)}, u32[]{:S(2)}) %all-to-all-start.3) | async-done | bytes 1572896 | tf_op jit(solution)/shard_map/all_to_all | solution.py:153
  332.5 5.6 %gather_fusion = bf16[1024,1536]{1,0:T(8,128)(2,1)} fusion(bf16[512,1536]{1,0:T(8,128)(2,1)S(1)} %bitcast.72, s32[1024]{0:T(1024)S(1)} %broadcast_clamp_fusion), kind=kCustom, calls=%fused_computation.1 | custom fusion | bytes 6295552 | tf_op jit(solution)/shard_map/gather | solution.py:155
  338.1 6.7 %reshape.453 = f32[256,4,1536]{2,1,0:T(4,128)} reshape(bf16[1024,1536]{1,0:T(8,128)(2,1)} %gather_fusion) | data formatting | bytes 9437184 | tf_op jit(solution)/shard_map/convert_element_type | solution.py:155
  344.8 7.4 %multiply_reduce_fusion = bf16[256,1536]{1,0:T(8,128)(2,1)S(1)} fusion(f32[256,4,1536]{2,1,0:T(4,128)} %reshape.453, f32[256,4]{1,0:T(8,128)S(1)} %copy.97), kind=kLoop, calls=%fused_computation.15 | loop fusion | flops 2752512 | bytes 7081984 | tf_op jit(solution)/shard_map/reduce_sum | solution.py:158
  352.9 15.7 %all_to_all.48 = bf16[256,4,384]{2,0,1:T(8,128)(2,1)S(1)} all-to-all(bf16[256,4,384]{2,0,1:T(8,128)(2,1)S(1)} %copy.99), channel_id=1, replica_groups=mesh['seq'=32,'mp'=4] {'mp'}, dimensions={1} | all-to-all | bytes 1572864 | tf_op jit(solution)/shard_map/all_to_all | solution.py:159
  (105 shorter events, 17.1 us)
Async XLA Ops:
  10.1 11.6 %copy-start.5 = (s32[256,4]{0,1:T(4,128)S(1)}, s32[256,4]{0,1:T(4,128)}, u32[]{:S(2)}) copy-start(s32[256,4]{0,1:T(4,128)} %param.15) | copy-start | bytes 12292
  10.1 12.0 %copy-start.6 = (s32[3]{0:T(128)S(1)}, s32[3]{0:T(128)}, u32[]{:S(2)}) copy-start(s32[3]{0:T(128)} %param.14) | copy-start | bytes 40
  10.1 16.0 %copy-start.2 = (bf16[256,384]{1,0:T(8,128)(2,1)S(1)}, bf16[256,384]{1,0:T(8,128)(2,1)}, u32[]{:S(2)}) copy-start(bf16[256,384]{1,0:T(8,128)(2,1)} %param.10) | copy-start | bytes 589828
  10.1 56.6 %all-to-all-start = ((bf16[32,48,1024]{2,1,0:T(8,128)(2,1)}), bf16[32,48,1024]{2,1,0:T(8,128)(2,1)}, u32[]{:S(2)}, u32[]{:S(2)}) async-start(bf16[32,48,1024]{2,1,0:T(8,128)(2,1)} %broadcast_in_dim.38), calls=%async_computation | async-start | bytes 6291456 | tf_op jit(solution)/shard_map/all_to_all | solution.py:44
  21.7 42.0 %copy-start.3 = (bf16[1,192,1536]{2,1,0:T(8,128)(2,1)S(1)}, bf16[1,192,1536]{2,1,0:T(8,128)(2,1)}, u32[]{:S(2)}) copy-start(bf16[1,192,1536]{2,1,0:T(8,128)(2,1)} %param.19) | copy-start | bytes 1769476
  62.3 0.9 copy-start
  70.2 5.6 %copy-start.1 = (bf16[256,1536]{1,0:T(8,128)(2,1)S(1)}, bf16[256,1536]{1,0:T(8,128)(2,1)}, u32[]{:S(2)}) copy-start(bf16[256,1536]{1,0:T(8,128)(2,1)} %copy-done) | copy-start | bytes 2359300
  70.3 191.6 %all-to-all-start.2 = ((bf16[4,3,192,1536]{3,2,1,0:T(8,128)(2,1)}), bf16[4,3,192,1536]{3,2,1,0:T(8,128)(2,1)}, u32[]{:S(2)}, u32[]{:S(2)}) async-start(bf16[4,3,192,1536]{3,2,1,0:T(8,128)(2,1)} %stack.2), calls=%async_computation.2 | async-start | bytes 14155776 | tf_op jit(solution)/shard_map/all_to_all | solution.py:60
  75.9 152.5 %reduce-scatter.4.cloned.1.call-start = ((), (), s32[]{:S(2)}) async-start(), calls=%async_computation.6 | async-start | bytes 983040
  78.9 23.1 %collective-permute-start = (bf16[256,256]{0,1:T(8,128)(2,1)S(1)}, bf16[256,256]{0,1:T(8,128)(2,1)}, u32[]{:S(2)}, u32[]{:S(2)}) collective-permute-start(bf16[256,256]{0,1:T(8,128)(2,1)S(1)} %pad_maximum_fusion.1), channel_id=1, source_target_pairs={{0,64},{4,68},{8,72},{12,76},{16,80},{20,84},{24,88},{28,92},{32,9... | collective-permute-start | bytes 393224 | tf_op jit(solution)/shard_map/ppermute | solution.py:86
  84.3 20.0 %collective-permute-start.1 = (bf16[256,256]{0,1:T(8,128)(2,1)S(1)}, bf16[256,256]{0,1:T(8,128)(2,1)}, u32[]{:S(2)}, u32[]{:S(2)}) collective-permute-start(bf16[256,256]{0,1:T(8,128)(2,1)S(1)} %pad_maximum_fusion.1), channel_id=1, source_target_pairs={{0,60},{4,64},{8,68},{12,72},{16,76},{20,80},{24,84},{28,88},{32,9... | collective-permute-start | bytes 393224 | tf_op jit(solution)/shard_map/ppermute | solution.py:86
  94.7 11.7 %collective-permute-start.2 = (bf16[256,256]{0,1:T(8,128)(2,1)S(1)}, bf16[256,256]{0,1:T(8,128)(2,1)}, u32[]{:S(2)}, u32[]{:S(2)}) collective-permute-start(bf16[256,256]{0,1:T(8,128)(2,1)S(1)} %pad_maximum_fusion.1), channel_id=1, source_target_pairs={{0,56},{4,60},{8,64},{12,68},{16,72},{20,76},{24,80},{28,84},{32,8... | collective-permute-start | bytes 393224 | tf_op jit(solution)/shard_map/ppermute | solution.py:86
  97.4 11.3 %collective-permute-start.3 = (bf16[256,256]{0,1:T(8,128)(2,1)S(1)}, bf16[256,256]{0,1:T(8,128)(2,1)}, u32[]{:S(2)}, u32[]{:S(2)}) collective-permute-start(bf16[256,256]{0,1:T(8,128)(2,1)S(1)} %pad_maximum_fusion.1), channel_id=1, source_target_pairs={{0,52},{4,56},{8,60},{12,64},{16,68},{20,72},{24,76},{28,80},{32,8... | collective-permute-start | bytes 393224 | tf_op jit(solution)/shard_map/ppermute | solution.py:86
  99.4 12.7 %collective-permute-start.4 = (bf16[256,256]{0,1:T(8,128)(2,1)S(1)}, bf16[256,256]{0,1:T(8,128)(2,1)}, u32[]{:S(2)}, u32[]{:S(2)}) collective-permute-start(bf16[256,256]{0,1:T(8,128)(2,1)S(1)} %pad_maximum_fusion.1), channel_id=1, source_target_pairs={{0,48},{4,52},{8,56},{12,60},{16,64},{20,68},{24,72},{28,76},{32,8... | collective-permute-start | bytes 393224 | tf_op jit(solution)/shard_map/ppermute | solution.py:86
  102.0 16.5 %collective-permute-start.5 = (bf16[256,256]{0,1:T(8,128)(2,1)S(1)}, bf16[256,256]{0,1:T(8,128)(2,1)S(1)}, u32[]{:S(2)}, u32[]{:S(2)}) collective-permute-start(bf16[256,256]{0,1:T(8,128)(2,1)S(1)} %pad_maximum_fusion.1), channel_id=1, source_target_pairs={{0,44},{4,48},{8,52},{12,56},{16,60},{20,64},{24,68},{28,72},{32,7... | collective-permute-start | bytes 393224 | tf_op jit(solution)/shard_map/ppermute | solution.py:86
  104.3 15.6 %collective-permute-start.6 = (bf16[256,256]{0,1:T(8,128)(2,1)S(1)}, bf16[256,256]{0,1:T(8,128)(2,1)S(1)}, u32[]{:S(2)}, u32[]{:S(2)}) collective-permute-start(bf16[256,256]{0,1:T(8,128)(2,1)S(1)} %pad_maximum_fusion.1), channel_id=1, source_target_pairs={{0,40},{4,44},{8,48},{12,52},{16,56},{20,60},{24,64},{28,68},{32,7... | collective-permute-start | bytes 393224 | tf_op jit(solution)/shard_map/ppermute | solution.py:86
  106.5 17.6 %collective-permute-start.7 = (bf16[256,256]{0,1:T(8,128)(2,1)S(1)}, bf16[256,256]{0,1:T(8,128)(2,1)S(1)}, u32[]{:S(2)}, u32[]{:S(2)}) collective-permute-start(bf16[256,256]{0,1:T(8,128)(2,1)S(1)} %pad_maximum_fusion.1), channel_id=1, source_target_pairs={{0,36},{4,40},{8,44},{12,48},{16,52},{20,56},{24,60},{28,64},{32,6... | collective-permute-start | bytes 393224 | tf_op jit(solution)/shard_map/ppermute | solution.py:86
  108.7 16.7 %collective-permute-start.8 = (bf16[256,256]{0,1:T(8,128)(2,1)S(1)}, bf16[256,256]{0,1:T(8,128)(2,1)S(1)}, u32[]{:S(2)}, u32[]{:S(2)}) collective-permute-start(bf16[256,256]{0,1:T(8,128)(2,1)S(1)} %pad_maximum_fusion.1), channel_id=1, source_target_pairs={{0,32},{4,36},{8,40},{12,44},{16,48},{20,52},{24,56},{28,60},{32,6... | collective-permute-start | bytes 393224 | tf_op jit(solution)/shard_map/ppermute | solution.py:86
  112.1 42.9 %collective-permute-start.9 = (bf16[256,256]{0,1:T(8,128)(2,1)S(1)}, bf16[256,256]{0,1:T(8,128)(2,1)S(1)}, u32[]{:S(2)}, u32[]{:S(2)}) collective-permute-start(bf16[256,256]{0,1:T(8,128)(2,1)S(1)} %pad_maximum_fusion.1), channel_id=1, source_target_pairs={{0,28},{4,32},{8,36},{12,40},{16,44},{20,48},{24,52},{28,56},{32,6... | collective-permute-start | bytes 393224 | tf_op jit(solution)/shard_map/ppermute | solution.py:86
  118.5 39.3 %collective-permute-start.10 = (bf16[256,256]{0,1:T(8,128)(2,1)S(1)}, bf16[256,256]{0,1:T(8,128)(2,1)S(1)}, u32[]{:S(2)}, u32[]{:S(2)}) collective-permute-start(bf16[256,256]{0,1:T(8,128)(2,1)S(1)} %pad_maximum_fusion.1), channel_id=1, source_target_pairs={{0,24},{4,28},{8,32},{12,36},{16,40},{20,44},{24,48},{28,52},{32,5... | collective-permute-start | bytes 393224 | tf_op jit(solution)/shard_map/ppermute | solution.py:86
  119.8 41.2 %collective-permute-start.11 = (bf16[256,256]{0,1:T(8,128)(2,1)S(1)}, bf16[256,256]{0,1:T(8,128)(2,1)S(1)}, u32[]{:S(2)}, u32[]{:S(2)}) collective-permute-start(bf16[256,256]{0,1:T(8,128)(2,1)S(1)} %pad_maximum_fusion.1), channel_id=1, source_target_pairs={{0,20},{4,24},{8,28},{12,32},{16,36},{20,40},{24,44},{28,48},{32,5... | collective-permute-start | bytes 393224 | tf_op jit(solution)/shard_map/ppermute | solution.py:86
  124.1 39.7 %collective-permute-start.12 = (bf16[256,256]{0,1:T(8,128)(2,1)S(1)}, bf16[256,256]{0,1:T(8,128)(2,1)S(1)}, u32[]{:S(2)}, u32[]{:S(2)}) collective-permute-start(bf16[256,256]{0,1:T(8,128)(2,1)S(1)} %pad_maximum_fusion.1), channel_id=1, source_target_pairs={{0,16},{4,20},{8,24},{12,28},{16,32},{20,36},{24,40},{28,44},{32,4... | collective-permute-start | bytes 393224 | tf_op jit(solution)/shard_map/ppermute | solution.py:86
  125.5 38.4 %collective-permute-start.13 = (bf16[256,256]{0,1:T(8,128)(2,1)S(1)}, bf16[256,256]{0,1:T(8,128)(2,1)S(1)}, u32[]{:S(2)}, u32[]{:S(2)}) collective-permute-start(bf16[256,256]{0,1:T(8,128)(2,1)S(1)} %pad_maximum_fusion.1), channel_id=1, source_target_pairs={{0,12},{4,16},{8,20},{12,24},{16,28},{20,32},{24,36},{28,40},{32,4... | collective-permute-start | bytes 393224 | tf_op jit(solution)/shard_map/ppermute | solution.py:86
  155.0 8.9 %collective-permute-start.14 = (bf16[256,256]{0,1:T(8,128)(2,1)S(1)}, bf16[256,256]{0,1:T(8,128)(2,1)S(1)}, u32[]{:S(2)}, u32[]{:S(2)}) collective-permute-start(bf16[256,256]{0,1:T(8,128)(2,1)S(1)} %pad_maximum_fusion.1), channel_id=1, source_target_pairs={{0,8},{4,12},{8,16},{12,20},{16,24},{20,28},{24,32},{28,36},{32,40... | collective-permute-start | bytes 393224 | tf_op jit(solution)/shard_map/ppermute | solution.py:86
  157.8 6.1 %collective-permute-start.15 = (bf16[256,256]{0,1:T(8,128)(2,1)S(1)}, bf16[256,256]{0,1:T(8,128)(2,1)S(1)}, u32[]{:S(2)}, u32[]{:S(2)}) collective-permute-start(bf16[256,256]{0,1:T(8,128)(2,1)S(1)} %pad_maximum_fusion.1), channel_id=1, source_target_pairs={{0,4},{4,8},{8,12},{12,16},{16,20},{20,24},{24,28},{28,32},{32,36}... | collective-permute-start | bytes 393224 | tf_op jit(solution)/shard_map/ppermute | solution.py:86
  261.9 32.3 %all-to-all-start.1 = ((bf16[32,16,1536]{2,1,0:T(8,128)(2,1)}), bf16[32,16,1536]{2,1,0:T(8,128)(2,1)S(1)}, u32[]{:S(2)}, u32[]{:S(2)}) async-start(bf16[32,16,1536]{2,1,0:T(8,128)(2,1)} %bitcast.18), calls=%async_computation.1 | async-start | bytes 3145728 | tf_op jit(solution)/shard_map/all_to_all | solution.py:140
  305.7 5.7 %copy-start.4 = (f32[256,4]{0,1:T(4,128)S(1)}, f32[256,4]{0,1:T(4,128)}, u32[]{:S(2)}) copy-start(f32[256,4]{0,1:T(4,128)} %param.16) | copy-start | bytes 12292
  305.7 26.8 %all-to-all-start.3 = ((bf16[32,16,1536]{2,1,0:T(8,128)(2,1)}), bf16[32,16,1536]{2,1,0:T(8,128)(2,1)S(1)}, u32[]{:S(2)}, u32[]{:S(2)}) async-start(bf16[32,16,1536]{2,1,0:T(8,128)(2,1)} %bitcast.78), calls=%async_computation.3 | async-start | bytes 3145728 | tf_op jit(solution)/shard_map/all_to_all | solution.py:153
Sparse Core Ops, SparseCore 0:
  189.5 38.8 reduce-scatter.3
